TPU v7x, 256 devices: a whole 4x4x8 slice. The times are simulated.
256 devices in a mesh: row: 32 (over z, y_hi, core), col: 8 (over y_lo, x).
Axes of the slice: x: 4, y: 4 (y_hi: 2, y_lo: 2; y = y_hi * 2 + y_lo), z: 8, core: 2. Of those that a mesh axis runs over, the one named last changes fastest.
Arguments:
- factor: float32 [49152, 8192], P('row', 'col'), may hold values from -0.0546875 to 0.0546875
- covariance: float32 [49152, 2048], P('row', 'col'), may hold values from -6 to 6
- inv_diagonal: float32 [8192], P(('col', 'row')), may hold values from 0.5 to 4
- columns: int32 [2048], replicated, may hold values from 0 to 8191
Outputs:
- sigma_window: float32 [8192, 2048], P(('col', 'row'))
Inputs may be any that keep to these rules, and one draw needn't show every extreme that they name: `columns`: each entry is a separator index; entries may repeat.
All inputs are finite; a program needn't handle non-finite values.
Results may differ from a plain program's by a relative error of at most 0.000071.
Values sent between devices are 32-bit elements; how exact they have to be, the bound alone decides.
No kernel may reach another device: no remote copies, remote signals or barrier semaphores. Data moves between devices by JAX's collectives and lax.ppermute only.
A program may use at most 128 MiB of HBM per device.

v0:
```python
import jax
import jax.numpy as jnp
from jax import lax
from jax.sharding import PartitionSpec as P


def contract_rows(left_block, right_block):
    return lax.dot_general(
        left_block,
        right_block,
        (((0,), (0,)), ((), ())),
        precision=lax.Precision.HIGHEST,
        preferred_element_type=jnp.float32,
    )


def per_device(factor, covariance, inv_diagonal, columns):
    row_devices = lax.axis_size("row")
    gathered = lax.all_gather(covariance, "col", axis=1, tiled=True)
    product = lax.psum_scatter(
        contract_rows(factor, gathered), "row", scatter_dimension=0, tiled=True
    )
    row_count = product.shape[0]
    block_index = lax.axis_index("col") * row_devices + lax.axis_index("row")
    row_ids = block_index * row_count + lax.iota(jnp.int32, row_count)
    on_diagonal = row_ids[:, None] == columns[None, :]
    return jnp.where(on_diagonal, inv_diagonal[:, None], jnp.zeros((), jnp.float32)) - product


def solution(mesh):
    return jax.shard_map(
        per_device,
        mesh=mesh,
        in_specs=(P("row", "col"), P("row", "col"), P(("col", "row")), P()),
        out_specs=P(("col", "row"), None),
        check_vma=False,
    )
```

profile of v0, /device:TPU:2, one launch (start us, length us, event | category | flops | bytes accessed | tf_op | source)
XLA Modules:
  0.0 352.7 jit_solution(8926620871789993303)
XLA Ops:
  6.5 0.0 all-gather.2.cloned.1.call-start
  6.5 0.7 all-gather.2.cloned.1.call-update
  7.3 0.0 reduce-scatter.2.cloned.1.call-start
  7.3 136.4 %all-gather.2.cloned.1.call-done = f32[1536,2048]{1,0:T(8,128)} async-done(((f32[1536,256]{1,0:T(8,128)}), f32[1536,2048]{1,0:T(8,128)}) %all-gather.2.cloned.1.call-update) | async-done | bytes 12582928 | tf_op jit(solution)/shard_map/all_gather | solution.py:19
  143.7 44.9 %fusion = f32[1024,2048]{1,0:T(8,128)} fusion(f32[1536,1024]{1,0:T(8,128)} %param.4, f32[1536,2048]{1,0:T(8,128)} %all-gather.2.cloned.1.call-done), kind=kOutput, calls=%fused_computation.2 | convolution fusion | flops 38654705664 | bytes 27262976 | tf_op jit(solution)/shard_map/dot_general | solution.py:8
  188.7 0.0 copy-start
  188.7 0.0 copy-start.1
  188.7 0.0 reduce-scatter.2.cloned.1.call-update
  188.7 155.3 %reduce-scatter.2.cloned.1.call-done = f32[32,2048]{1,0:T(8,128)} async-done(((f32[1024,2048]{1,0:T(8,128)}), f32[32,2048]{1,0:T(8,128)}) %reduce-scatter.2.cloned.1.call-update) | async-done | bytes 262160 | tf_op jit(solution)/shard_map/reduce_scatter | solution.py:20
  344.1 0.0 copy-done
  344.1 0.0 copy-done.1
  344.1 1.7 select_subtract_fusion
  (1 shorter events, 0.0 us)
Async XLA Ops:
  6.5 137.2 %all-gather.2.cloned.1.call-start = ((), (), s32[]{:S(2)}) async-start(), calls=%async_computation.1 | async-start | bytes 14155776 | tf_op jit(solution)/shard_map/all_gather | solution.py:19
  7.3 336.8 %reduce-scatter.2.cloned.1.call-start = ((), (), s32[]{:S(2)}) async-start(), calls=%async_computation.2 | async-start | bytes 8650752 | tf_op jit(solution)/shard_map/reduce_scatter | solution.py:20
  188.7 155.4 %copy-start = (s32[2048]{0:T(1024)S(1)}, s32[2048]{0:T(1024)}, u32[]{:S(2)}) copy-start(s32[2048]{0:T(1024)} %param.7) | copy-start | bytes 24580
  188.7 155.4 %copy-start.1 = (f32[32]{0:T(128)S(1)}, f32[32]{0:T(128)}, u32[]{:S(2)}) copy-start(f32[32]{0:T(128)} %param.6) | copy-start | bytes 388
Sparse Core Ops, SparseCore 0:
  9.1 134.5 all-gather.1
  188.8 155.1 reduce-scatter.1
where the time goes:
time: 353 us
  waiting for transfers between devices  292 us (83%)
  matrix products  44.9 us (13%)
  between operations  13.4 us (4%)
    reduce_scatter x1, waiting for transfers between devices, per_device(): lax.psum_scatter(contract_rows(factor, gathered), 'row', scatter_dimensio...  155 us
    all_gather x1, waiting for transfers between devices, per_device(): gathered = lax.all_gather(covariance, 'col', axis=1, tiled=True)  136 us
    dot_general x1, matrix products, contract_rows(): lax.dot_general(left_block, right_block, (((0,), (0,)), ((), ())), precis...  44.9 us
  transfers between devices with their start and end apart: 2, of which 2 were waited for; matrix products, arithmetic and copies ran while one was open for 0% of the time, Pallas kernels for 0%

commit v1 on v0

--- a/solution.py
+++ b/solution.py
@@ -2,6 +2,11 @@
 import jax.numpy as jnp
 from jax import lax
 from jax.sharding import PartitionSpec as P
+
+
+def exchange_gather(block, axis, along):
+    sent = jnp.stack([block] * lax.axis_size(axis))
+    return jnp.concatenate(lax.all_to_all(sent, axis, 0, 0), axis=along)
 
 
 def contract_rows(left_block, right_block):
@@ -16,7 +21,7 @@
 
 def per_device(factor, covariance, inv_diagonal, columns):
     row_devices = lax.axis_size("row")
-    gathered = lax.all_gather(covariance, "col", axis=1, tiled=True)
+    gathered = exchange_gather(covariance, "col", 1)
     product = lax.psum_scatter(
         contract_rows(factor, gathered), "row", scatter_dimension=0, tiled=True
     )

time: 353 us -> 402 us (1.14)
  blocking collectives: 0 us -> 146 us
  waiting for transfers between devices: 292 us -> 156 us
  matrix products: 44.9 us -> 82 us
    all_to_all x0 -> x1, blocking collectives: none -> 146 us  [exchange_gather(): return jnp.concatenate(lax.all_to_all(sent, axis, 0, 0), axis=along)]
    all_gather x1 -> x0, waiting for transfers between devices: 136 us -> none  [per_device(): gathered = lax.all_gather(covariance, 'col', axis=1, tiled=True)]
    dot_general x1, matrix products: 44.9 us -> 82 us  [contract_rows(): lax.dot_general(left_block, right_block, (((0,), (0,)), ((), ())), precis...]
  transfers between devices with their start and end apart: 2 -> 1, of which waited for: 2 -> 1; matrix products, arithmetic and copies ran while one was open for 0% -> 0% of each run, Pallas kernels for 0% -> 0%
where the time goes in v1:
time: 402 us
  waiting for transfers between devices  156 us (39%)
  blocking collectives  146 us (36%)
  matrix products  82 us (20%)
  between operations  13.4 us (3%)
    reduce_scatter x1, waiting for transfers between devices, per_device(): lax.psum_scatter(contract_rows(factor, gathered), 'row', scatter_dimensio...  156 us
    all_to_all x1, blocking collectives, exchange_gather(): return jnp.concatenate(lax.all_to_all(sent, axis, 0, 0), axis=along)  146 us
    dot_general x1, matrix products, contract_rows(): lax.dot_general(left_block, right_block, (((0,), (0,)), ((), ())), precis...  82 us
  transfers between devices with their start and end apart: 1, of which 1 were waited for; matrix products, arithmetic and copies ran while one was open for 0% of the time, Pallas kernels for 0%

profile of v1, /device:TPU:2, one launch (start us, length us, event | category | flops | bytes accessed | tf_op | source)
XLA Modules:
  0.0 402.1 jit_solution(17100753431786356676)
XLA Ops:
  6.5 0.0 reduce-scatter.2.cloned.1.call-start
  6.5 1.9 copy.5
  8.4 1.6 stack.2
  10.0 145.7 %all_to_all.5 = f32[8,1536,256]{1,2,0:T(8,128)S(1)} all-to-all(f32[8,1536,256]{1,2,0:T(8,128)S(1)} %stack.2), channel_id=1, replica_groups=mesh['row'=32,'col'=8] {'col'}, dimensions={0} | all-to-all | bytes 25165824 | tf_op jit(solution)/shard_map/all_to_all | solution.py:9
  155.8 82.0 %fusion = f32[1024,2048]{1,0:T(8,128)} fusion(f32[1536,1024]{1,0:T(8,128)} %param.4, f32[1536,2048]{0,1:T(8,128)S(1)} %bitcast.5), kind=kOutput, calls=%fused_computation.2 | convolution fusion | flops 38654705664 | bytes 27262976 | tf_op jit(solution)/shard_map/dot_general | solution.py:13
  237.7 0.0 copy-start
  237.7 0.0 copy-start.1
  237.7 0.0 reduce-scatter.2.cloned.1.call-update
  237.8 155.7 %reduce-scatter.2.cloned.1.call-done = f32[32,2048]{1,0:T(8,128)} async-done(((f32[1024,2048]{1,0:T(8,128)}), f32[32,2048]{1,0:T(8,128)}) %reduce-scatter.2.cloned.1.call-update) | async-done | bytes 262160 | tf_op jit(solution)/shard_map/reduce_scatter | solution.py:25
  393.5 0.0 copy-done
  393.5 0.0 copy-done.1
  393.5 1.7 select_subtract_fusion
  (1 shorter events, 0.0 us)
Async XLA Ops:
  6.5 386.9 %reduce-scatter.2.cloned.1.call-start = ((), (), s32[]{:S(2)}) async-start(), calls=%async_computation.2 | async-start | bytes 8650752 | tf_op jit(solution)/shard_map/reduce_scatter | solution.py:25
  237.7 155.7 %copy-start = (s32[2048]{0:T(1024)S(1)}, s32[2048]{0:T(1024)}, u32[]{:S(2)}) copy-start(s32[2048]{0:T(1024)} %param.7) | copy-start | bytes 24580
  237.7 155.7 %copy-start.1 = (f32[32]{0:T(128)S(1)}, f32[32]{0:T(128)}, u32[]{:S(2)}) copy-start(f32[32]{0:T(128)} %param.6) | copy-start | bytes 388
Sparse Core Ops, SparseCore 0:
  237.9 155.5 reduce-scatter.1
